TPU v7x, 128 devices: a whole 4x4x4 slice. The times are simulated.
128 devices in a mesh: fsdp: 8 (over x, z_lo), dp: 16 (over z_hi, y, core).
Axes of the slice: x: 4, y: 4, z: 4 (z_hi: 2, z_lo: 2; z = z_hi * 2 + z_lo), core: 2. Of those that a mesh axis runs over, the one named last changes fastest.
Arguments:
- tokens: bfloat16 [8, 2176, 3200], P('fsdp', 'dp'), may hold values from -6 to 6
- norm_gain: float32 [3200], replicated, may hold values from 0.5 to 1.5
- qkv_weight: bfloat16 [3200, 6144], P('fsdp', 'dp'), may hold values from -4 to 4
- qk_gain: float32 [2, 2048], P(None, 'dp'), may hold values from 1 to 8
- out_weight: bfloat16 [2048, 3200], P('dp', 'fsdp'), may hold values from -0.125 to 0.125
- layer_scale: float32 [3200], replicated, may hold values from 0.2 to 1
- tile_counts: int32 [8, 2], replicated, may hold values from 0 to 2, as said below
- owners: int32 [8, 2], replicated, may hold values from 0 to 7, as said below
Outputs:
- vision_tokens: bfloat16 [32, 256, 12800], P('fsdp', None, 'dp')
Inputs may be any that keep to these rules, and one draw needn't show every extreme that they name: `tile_counts`: column 0 is 1 to 2, column 1 is 0 to 2 minus column 0. All owners together get at most 4 live tiles each, and one owner gets exactly 4.
All inputs are finite; a program needn't handle non-finite values.
Results may differ from a plain program's by a relative error of at most 0.006.
The roundings to bfloat16 on the way count: a program that leaves them out, or rounds other values in their place, can miss the bound.
Values may be sent and summed in bfloat16 or wider, within the bound.
No kernel may reach another device: no remote copies, remote signals or barrier semaphores. Data moves between devices by JAX's collectives and lax.ppermute only.
A program may use at most 192 MiB of HBM per device.

v0:
```python
import jax
import jax.numpy as jnp
from jax import lax
from jax.sharding import PartitionSpec as P

HEAD_DIM = 128
GRID = 32
SLOTS = 2
TILE = 1025
CAP = 4
EPSILON = 1e-06


def merge_tiles(values):
    halves = GRID // 2
    columns = values.shape[1]
    tile_list = []
    for tile_slot in range(SLOTS):
        patches = values[tile_slot * TILE + 1 : (tile_slot + 1) * TILE]
        square = patches.reshape(halves, 2, halves, 2, columns).transpose(0, 2, 4, 1, 3)
        tile_list.append(square.reshape(halves * halves, columns * 4))
    return jnp.stack(tile_list)


def tile_owners(tile_counts, owners):
    slot_index = jnp.arange(SLOTS, dtype=jnp.int32)[None, :]
    first_count = tile_counts[:, 0:1]
    holder = jnp.where(slot_index < first_count, owners[:, 0:1], owners[:, 1:2])
    living = slot_index < first_count + tile_counts[:, 1:2]
    return (holder, living)


def place_tiles(received, holder, living, target):
    owned_flag = jnp.logical_and(living, holder == target).reshape(-1).astype(jnp.int32)
    before = jnp.cumsum(owned_flag) - owned_flag
    chosen = jnp.logical_and(
        before[None, :] == jnp.arange(CAP, dtype=jnp.int32)[:, None], owned_flag[None, :] == 1
    )
    flattened = received.reshape(received.shape[0] * received.shape[1], -1)
    placed = jnp.dot(chosen.astype(jnp.bfloat16), flattened, preferred_element_type=jnp.float32)
    return placed.astype(jnp.bfloat16).reshape(CAP, received.shape[2], received.shape[3])


def body(tokens, norm_gain, qkv_weight, qk_gain, out_weight, layer_scale, tile_counts, owners):
    own_rows = tokens[0]
    gathered = lax.all_gather(own_rows, "dp", axis=0, tiled=True)
    length = gathered.shape[0]
    model_width = gathered.shape[1]
    groups = lax.axis_size("dp")
    values = gathered.astype(jnp.float32)
    normed = (
        values * lax.rsqrt(jnp.mean(values * values, axis=-1, keepdims=True) + EPSILON) * norm_gain
    ).astype(jnp.bfloat16)
    projected = jnp.dot(
        normed,
        lax.all_gather(qkv_weight, "fsdp", axis=0, tiled=True),
        preferred_element_type=jnp.float32,
    )
    queries = projected[:, :HEAD_DIM]
    keys_part = projected[:, HEAD_DIM : 2 * HEAD_DIM]
    values_part = projected[:, 2 * HEAD_DIM :].astype(jnp.bfloat16)
    query_sums, key_sums = lax.psum(
        (jnp.sum(queries * queries, axis=-1), jnp.sum(keys_part * keys_part, axis=-1)), "dp"
    )
    window = groups * HEAD_DIM
    queries = (queries * lax.rsqrt(query_sums / window + EPSILON)[:, None] * qk_gain[0]).astype(
        jnp.bfloat16
    )
    keys_part = (keys_part * lax.rsqrt(key_sums / window + EPSILON)[:, None] * qk_gain[1]).astype(
        jnp.bfloat16
    )
    row_index = lax.axis_index("fsdp")
    row_count = lax.axis_size("fsdp")
    factor = HEAD_DIM ** (-0.5)
    covered = SLOTS * TILE
    tile_query = queries[:covered].reshape(SLOTS, TILE, HEAD_DIM)
    tile_key = keys_part[:covered].reshape(SLOTS, TILE, HEAD_DIM)
    tile_value = values_part[:covered].reshape(SLOTS, TILE, HEAD_DIM)
    scores = (
        jnp.einsum("sqc,skc->sqk", tile_query, tile_key, preferred_element_type=jnp.float32)
        * factor
    )
    highest = jnp.max(scores, axis=-1, keepdims=True)
    exponent = jnp.exp(scores - highest)
    weights = (exponent / jnp.sum(exponent, axis=-1, keepdims=True)).astype(jnp.bfloat16)
    tile_out = jnp.einsum(
        "sqk,skc->sqc", weights, tile_value, preferred_element_type=jnp.float32
    ).astype(jnp.bfloat16)
    head_out = jnp.concatenate(
        [
            tile_out.reshape(covered, HEAD_DIM),
            jnp.zeros((length - covered, HEAD_DIM), jnp.bfloat16),
        ],
        axis=0,
    )
    dp_index = lax.axis_index("dp")
    block = model_width // groups
    head_rows = lax.all_gather(out_weight, "fsdp", axis=1, tiled=True)
    weight_block = lax.all_to_all(head_rows, "dp", split_axis=1, concat_axis=0, tiled=True)
    all_heads = lax.all_gather(head_out, "dp", axis=0, tiled=False)
    head_terms = jnp.einsum(
        "hsc,hcd->hsd",
        all_heads,
        weight_block.reshape(groups, HEAD_DIM, block),
        preferred_element_type=jnp.float32,
    ).astype(jnp.bfloat16)
    attention = jnp.sum(lax.optimization_barrier(head_terms).astype(jnp.float32), axis=0)
    own_block = lax.dynamic_slice_in_dim(gathered, dp_index * block, block, axis=1)
    scale_block = lax.dynamic_slice_in_dim(layer_scale, dp_index * block, block)
    updated = (own_block.astype(jnp.float32) + scale_block * attention).astype(jnp.bfloat16)
    merged = merge_tiles(updated)
    holder, living = tile_owners(tile_counts, owners)
    own_holder = holder[row_index]
    own_living = living[row_index]
    destination = jnp.arange(row_count, dtype=jnp.int32)[:, None]
    sending = jnp.logical_and(destination == own_holder[None, :], own_living[None, :])
    outgoing = jnp.where(sending[:, :, None, None], merged[None], jnp.zeros((), jnp.bfloat16))
    received = lax.all_to_all(outgoing, "fsdp", split_axis=0, concat_axis=0, tiled=True)
    return place_tiles(received, holder, living, row_index)


def solution(mesh):
    placed = (
        P("fsdp", "dp", None),
        P(),
        P("fsdp", "dp"),
        P(None, "dp"),
        P("dp", "fsdp"),
        P(),
        P(),
        P(),
    )
    return jax.shard_map(
        body, mesh=mesh, in_specs=placed, out_specs=P("fsdp", None, "dp"), check_vma=False
    )
```

profile of v0, /device:TPU:1, one launch (start us, length us, event | category | flops | bytes accessed | tf_op | source)
XLA Modules:
  0.0 529.9 jit_solution(8321030742287554255)
XLA Ops:
  8.8 101.3 %all-gather.8.cloned.1.call-done = bf16[1,2176,3200]{2,1,0:T(8,128)(2,1)} async-done(((bf16[1,136,3200]{2,1,0:T(8,128)(2,1)}), bf16[1,2176,3200]{2,1,0:T(8,128)(2,1)}) %all-gather.8.cloned.1.call-update) | async-done | bytes 13926416 | tf_op jit(solution)/shard_map/all_gather | solution.py:46
  110.2 7.7 %fusion.1 = f32[2176]{0:T(1024)S(1)} fusion(bf16[1,2176,3200]{2,1,0:T(8,128)(2,1)} %all-gather.8.cloned.1.call-done), kind=kLoop, calls=%fused_computation.4 | loop fusion | flops 20887424 | bytes 13935104 | tf_op jit(solution)/shard_map/reduce_sum | solution.py:52
  117.9 47.7 %all-gather.6.cloned.1.call-done = bf16[3200,384]{1,0:T(8,128)(2,1)} async-done(((bf16[400,384]{1,0:T(8,128)(2,1)}), bf16[3200,384]{1,0:T(8,128)(2,1)}) %all-gather.6.cloned.1.call-update) | async-done | bytes 2457616 | tf_op jit(solution)/shard_map/all_gather | solution.py:56
  165.6 11.8 %fusion.5 = f32[2176,384]{1,0:T(8,128)S(1)} fusion(bf16[3200,384]{1,0:T(8,128)(2,1)} %all-gather.6.cloned.1.call-done, bf16[1,2176,3200]{2,1,0:T(8,128)(2,1)} %all-gather.8.cloned.1.call-done, f32[3200]{0:T(1024)S(1)} %copy-done.4, f32[2176]{0:T(1024)S(1)} %add_rsqrt_fusion.2), kind=kOutput, calls=%fused_computation.11 | convolution fusion | flops 5375590400 | bytes 19747840 | tf_op jit(solution)/shard_map/dot_general | solution.py:54
  178.2 65.0 %all-reduce.1 = (f32[2176]{0:T(1024)S(1)}, f32[2176]{0:T(1024)S(1)}) all-reduce(f32[2176]{0:T(1024)S(1)} %get-tuple-element.6, f32[2176]{0:T(1024)S(1)} %get-tuple-element.5), channel_id=1, replica_groups=mesh['fsdp'=8,'dp'=16] {'dp'}, use_global_device_ids=true, to_apply=%region_3.0 | all-reduce | flops 4352 | bytes 34816 | tf_op jit(solution)/shard_map/psum | solution.py:62
  245.5 3.2 fusion.32
  248.7 4.9 fusion.12
  254.6 27.5 %all_gather.19 = bf16[128,3200]{0,1:T(8,128)(2,1)} all-gather(bf16[128,400]{0,1:T(8,128)(2,1)S(1)} %copy-done.1), channel_id=1, replica_groups=mesh['fsdp'=8,'dp'=16] {'fsdp'}, dimensions={1}, use_global_device_ids=true | all-gather | bytes 921600 | tf_op jit(solution)/shard_map/all_gather | solution.py:98
  282.1 15.1 %all-to-all-start = ((bf16[128,16,200]{0,2,1:T(8,128)(2,1)}), bf16[128,16,200]{0,2,1:T(8,128)(2,1)S(1)}, u32[]{:S(2)}, u32[]{:S(2)}) async-start(bf16[128,16,200]{0,2,1:T(8,128)(2,1)} %bitcast.12), calls=%async_computation | async-start | bytes 1638400 | tf_op jit(solution)/shard_map/all_to_all | solution.py:99
  301.5 14.2 %all-to-all-done = bf16[128,16,200]{0,2,1:T(8,128)(2,1)S(1)} async-done(((bf16[128,16,200]{0,2,1:T(8,128)(2,1)}), bf16[128,16,200]{0,2,1:T(8,128)(2,1)S(1)}, u32[]{:S(2)}, u32[]{:S(2)}) %all-to-all-start) | async-done | bytes 819232 | tf_op jit(solution)/shard_map/all_to_all | solution.py:99
  315.7 31.7 %all-gather.10.cloned.1.call-done = bf16[34816,128]{1,0:T(8,128)(2,1)} async-done(((bf16[2176,128]{1,0:T(8,128)(2,1)}), bf16[34816,128]{1,0:T(8,128)(2,1)}) %all-gather.10.cloned.1.call-update) | async-done | bytes 8912912 | tf_op jit(solution)/shard_map/all_gather | solution.py:100
  347.3 10.8 %convolution_convert_fusion.1 = bf16[16,2176,200]{1,2,0:T(8,128)(2,1)} fusion(bf16[16,2176,128]{2,1,0:T(8,128)(2,1)} %bitcast.53, bf16[128,16,200]{0,2,1:T(8,128)(2,1)S(1)} %all-to-all-done), kind=kOutput, calls=%fused_computation.8 | convolution fusion | flops 1789542400 | bytes 23658496 | tf_op jit(solution)/shard_map/hsc,hcd->hsd/dot_general | solution.py:101
  358.2 7.3 %convert_reduce_fusion = f32[2176,200]{0,1:T(8,128)S(1)} fusion(bf16[16,2176,200]{1,2,0:T(8,128)(2,1)} %convolution_convert_fusion.1), kind=kLoop, calls=%fused_computation.7 | loop fusion | flops 13491200 | bytes 15667200 | tf_op jit(solution)/shard_map/reduce_sum | solution.py:107
  368.7 4.9 copy.33
  373.5 3.9 stack_reshape.7
  377.4 4.9 copy.31
  382.3 3.8 stack_reshape.6
  387.3 3.3 broadcast_select_fusion
  390.7 5.0 all-to-all-start.1
  396.0 90.6 %all-to-all-done.1 = bf16[8,2,256,800]{2,3,1,0:T(8,128)(2,1)} async-done(((bf16[8,2,256,800]{2,3,1,0:T(8,128)(2,1)}), bf16[8,2,256,800]{2,3,1,0:T(8,128)(2,1)}, u32[]{:S(2)}, u32[]{:S(2)}) %all-to-all-start.1) | async-done | bytes 6553632 | tf_op jit(solution)/shard_map/all_to_all | solution.py:118
  486.6 11.1 %copy.34 = bf16[8,2,256,800]{3,2,1,0:T(8,128)(2,1)} copy(bf16[8,2,256,800]{2,3,1,0:T(8,128)(2,1)} %all-to-all-done.1) | data formatting | bytes 13107200 | tf_op jit(solution)/shard_map/all_to_all | solution.py:118
  497.7 14.7 %reshape.247 = bf16[16,204800]{1,0:T(8,128)(2,1)} reshape(bf16[8,2,256,800]{3,2,1,0:T(8,128)(2,1)} %copy.34) | data formatting | bytes 13107200 | tf_op jit(solution)/shard_map/reshape | solution.py:39
  512.4 4.0 convolution_convert_fusion
  518.0 2.8 reshape.248
  (52 shorter events, 19.1 us)
Async XLA Ops:
  6.5 103.6 %all-gather.8.cloned.1.call-start = ((), (), s32[]{:S(2)}) async-start(), calls=%async_computation.3 | async-start | bytes 14796800 | tf_op jit(solution)/shard_map/all_gather | solution.py:46
  7.3 158.4 %all-gather.6.cloned.1.call-start = ((), (), s32[]{:S(2)}) async-start(), calls=%async_computation.2 | async-start | bytes 2764800 | tf_op jit(solution)/shard_map/all_gather | solution.py:56
  8.0 339.3 %all-gather.10.cloned.1.call-start = ((), (), s32[]{:S(2)}) async-start(), calls=%async_computation.4 | async-start | bytes 9469952 | tf_op jit(solution)/shard_map/all_gather | solution.py:100
  8.8 156.8 %copy-start.4 = (f32[3200]{0:T(1024)S(1)}, f32[3200]{0:T(1024)}, u32[]{:S(2)}) copy-start(f32[3200]{0:T(1024)} %param.9) | copy-start | bytes 38404
  245.3 3.4 copy-start
  248.7 5.9 %copy-start.1 = (bf16[128,400]{0,1:T(8,128)(2,1)S(1)}, bf16[128,400]{0,1:T(8,128)(2,1)}, u32[]{:S(2)}) copy-start(bf16[128,400]{0,1:T(8,128)(2,1)} %param.12) | copy-start | bytes 307204
  248.7 48.5 %copy-start.2 = (s32[8,2]{0,1:T(2,128)S(1)}, s32[8,2]{0,1:T(2,128)}, u32[]{:S(2)}) copy-start(s32[8,2]{0,1:T(2,128)} %param.15) | copy-start | bytes 196
  248.7 48.5 %copy-start.3 = (s32[8,2]{0,1:T(2,128)S(1)}, s32[8,2]{0,1:T(2,128)}, u32[]{:S(2)}) copy-start(s32[8,2]{0,1:T(2,128)} %param.14) | copy-start | bytes 196
  282.1 33.6 %all-to-all-start = ((bf16[128,16,200]{0,2,1:T(8,128)(2,1)}), bf16[128,16,200]{0,2,1:T(8,128)(2,1)S(1)}, u32[]{:S(2)}, u32[]{:S(2)}) async-start(bf16[128,16,200]{0,2,1:T(8,128)(2,1)} %bitcast.12), calls=%async_computation | async-start | bytes 1638400 | tf_op jit(solution)/shard_map/all_to_all | solution.py:99
  390.7 95.9 %all-to-all-start.1 = ((bf16[8,2,256,800]{2,3,1,0:T(8,128)(2,1)}), bf16[8,2,256,800]{2,3,1,0:T(8,128)(2,1)}, u32[]{:S(2)}, u32[]{:S(2)}) async-start(bf16[8,2,256,800]{2,3,1,0:T(8,128)(2,1)} %broadcast_select_fusion), calls=%async_computation.1 | async-start | bytes 13107200 | tf_op jit(solution)/shard_map/all_to_all | solution.py:118
Sparse Core Ops, SparseCore 0:
  9.8 100.3 all-gather.7
  111.8 53.8 all-gather.5
  254.7 92.5 all-gather.9
where the time goes:
time: 535 us; the launch traced here: 530 us
  waiting for transfers between devices  287 us (54%)
  blocking collectives  92.5 us (17%)
  local copies, waits for them, and re-layouts  59.9 us (11%)
  matrix products  34.7 us (6%)
  other arithmetic  22 us (4%)
  starting transfers between devices  20.1 us (4%)
  between operations  13.6 us (3%)
    all_gather x1, waiting for transfers between devices, body(): gathered = lax.all_gather(own_rows, 'dp', axis=0, tiled=True)  101 us
    all_to_all x1, waiting for transfers between devices, body(): lax.all_to_all(outgoing, 'fsdp', split_axis=0, concat_axis=0, tiled=True)  90.6 us
    psum x1, blocking collectives, body(): lax.psum((jnp.sum(queries * queries, axis=-1), jnp.sum(keys_part * keys_p...  65 us
    all_gather x1, waiting for transfers between devices, body(): lax.all_gather(qkv_weight, 'fsdp', axis=0, tiled=True)  47.7 us
    all_gather x1, waiting for transfers between devices, body(): all_heads = lax.all_gather(head_out, 'dp', axis=0, tiled=False)  31.7 us
    all_gather x1, blocking collectives, body(): head_rows = lax.all_gather(out_weight, 'fsdp', axis=1, tiled=True)  27.5 us
    all_to_all x1, starting transfers between devices, body(): lax.all_to_all(head_rows, 'dp', split_axis=1, concat_axis=0, tiled=True)  15.1 us
    reshape x1, local copies, waits for them, and re-layouts, place_tiles(): flattened = received.reshape(received.shape[0] * received.shape[1], -1)  14.7 us
  transfers between devices with their start and end apart: 5, of which 5 were waited for; matrix products, arithmetic and copies ran while one was open for 2% of the time, Pallas kernels for 0%

commit v1 on v0

--- a/solution.py
+++ b/solution.py
@@ -96,7 +96,10 @@
     dp_index = lax.axis_index("dp")
     block = model_width // groups
     head_rows = lax.all_gather(out_weight, "fsdp", axis=1, tiled=True)
-    weight_block = lax.all_to_all(head_rows, "dp", split_axis=1, concat_axis=0, tiled=True)
+    weight_block = jnp.concatenate(
+        lax.all_to_all(jnp.stack(jnp.split(head_rows, lax.axis_size("dp"), axis=1)), "dp", 0, 0),
+        axis=0,
+    )
     all_heads = lax.all_gather(head_out, "dp", axis=0, tiled=False)
     head_terms = jnp.einsum(
         "hsc,hcd->hsd",

time: 535 us -> 535 us (level)
  local copies, waits for them, and re-layouts: 59.9 us -> 69.4 us
  waiting for transfers between devices: 287 us -> 279 us
    unnamed x12 -> x27, local copies, waits for them, and re-layouts: 2.47 us -> 11.8 us
    all_gather x1, waiting for transfers between devices: 31.7 us -> 25.5 us  [body(): all_heads = lax.all_gather(head_out, 'dp', axis=0, tiled=False)]
  transfers between devices with their start and end apart: 5 -> 5, of which waited for: 5 -> 5; matrix products, arithmetic and copies ran while one was open for 2% -> 4% of each run, Pallas kernels for 0% -> 0%
where the time goes in v1:
time: 535 us; the launch traced here: 529 us
  waiting for transfers between devices  279 us (52%)
  blocking collectives  90.4 us (17%)
  local copies, waits for them, and re-layouts  69.4 us (13%)
  matrix products  34.7 us (6%)
  other arithmetic  22 us (4%)
  starting transfers between devices  20.6 us (4%)
  between operations  13.6 us (3%)
    all_gather x1, waiting for transfers between devices, body(): gathered = lax.all_gather(own_rows, 'dp', axis=0, tiled=True)  101 us
    all_to_all x1, waiting for transfers between devices, body(): lax.all_to_all(outgoing, 'fsdp', split_axis=0, concat_axis=0, tiled=True)  90.6 us
    psum x1, blocking collectives, body(): lax.psum((jnp.sum(queries * queries, axis=-1), jnp.sum(keys_part * keys_p...  65 us
    all_gather x1, waiting for transfers between devices, body(): lax.all_gather(qkv_weight, 'fsdp', axis=0, tiled=True)  47.7 us
    all_gather x1, waiting for transfers between devices, body(): all_heads = lax.all_gather(head_out, 'dp', axis=0, tiled=False)  25.5 us
    all_gather x1, blocking collectives, body(): head_rows = lax.all_gather(out_weight, 'fsdp', axis=1, tiled=True)  25.4 us
    all_to_all x1, starting transfers between devices, body(): lax.all_to_all(jnp.stack(jnp.split(head_rows, lax.axis_size('dp'), axis=1...  15.6 us
    reshape x1, local copies, waits for them, and re-layouts, place_tiles(): flattened = received.reshape(received.shape[0] * received.shape[1], -1)  14.7 us
  transfers between devices with their start and end apart: 5, of which 5 were waited for; matrix products, arithmetic and copies ran while one was open for 4% of the time, Pallas kernels for 0%

profile of v1, /device:TPU:1, one launch (start us, length us, event | category | flops | bytes accessed | tf_op | source)
XLA Modules:
  0.0 529.3 jit_solution(11174070470616331768)
XLA Ops:
  8.8 101.3 %all-gather.8.cloned.1.call-done = bf16[1,2176,3200]{2,1,0:T(8,128)(2,1)} async-done(((bf16[1,136,3200]{2,1,0:T(8,128)(2,1)}), bf16[1,2176,3200]{2,1,0:T(8,128)(2,1)}) %all-gather.8.cloned.1.call-update) | async-done | bytes 13926416 | tf_op jit(solution)/shard_map/all_gather | solution.py:46
  110.2 7.7 %fusion.1 = f32[2176]{0:T(1024)S(1)} fusion(bf16[1,2176,3200]{2,1,0:T(8,128)(2,1)} %all-gather.8.cloned.1.call-done), kind=kLoop, calls=%fused_computation.4 | loop fusion | flops 20887424 | bytes 13935104 | tf_op jit(solution)/shard_map/reduce_sum | solution.py:52
  117.9 47.7 %all-gather.6.cloned.1.call-done = bf16[3200,384]{1,0:T(8,128)(2,1)} async-done(((bf16[400,384]{1,0:T(8,128)(2,1)}), bf16[3200,384]{1,0:T(8,128)(2,1)}) %all-gather.6.cloned.1.call-update) | async-done | bytes 2457616 | tf_op jit(solution)/shard_map/all_gather | solution.py:56
  165.6 11.8 %fusion.5 = f32[2176,384]{1,0:T(8,128)S(1)} fusion(bf16[3200,384]{1,0:T(8,128)(2,1)} %all-gather.6.cloned.1.call-done, bf16[1,2176,3200]{2,1,0:T(8,128)(2,1)} %all-gather.8.cloned.1.call-done, f32[3200]{0:T(1024)S(1)} %copy-done.4, f32[2176]{0:T(1024)S(1)} %add_rsqrt_fusion.2), kind=kOutput, calls=%fused_computation.11 | convolution fusion | flops 5375590400 | bytes 19747840 | tf_op jit(solution)/shard_map/dot_general | solution.py:54
  178.2 65.0 %all-reduce.1 = (f32[2176]{0:T(1024)S(1)}, f32[2176]{0:T(1024)S(1)}) all-reduce(f32[2176]{0:T(1024)S(1)} %get-tuple-element.6, f32[2176]{0:T(1024)S(1)} %get-tuple-element.5), channel_id=1, replica_groups=mesh['fsdp'=8,'dp'=16] {'dp'}, use_global_device_ids=true, to_apply=%region_3.0 | all-reduce | flops 4352 | bytes 34816 | tf_op jit(solution)/shard_map/psum | solution.py:62
  245.5 3.2 fusion.47
  248.7 4.9 fusion.12
  254.6 25.4 %all_gather.19 = bf16[128,3200]{0,1:T(8,128)(2,1)S(1)} all-gather(bf16[128,400]{0,1:T(8,128)(2,1)S(1)} %copy-done.1), channel_id=1, replica_groups=mesh['fsdp'=8,'dp'=16] {'fsdp'}, dimensions={1}, use_global_device_ids=true | all-gather | bytes 921600 | tf_op jit(solution)/shard_map/all_gather | solution.py:98
  290.0 15.6 %all-to-all-start = ((bf16[16,128,200]{1,2,0:T(8,128)(2,1)}), bf16[16,128,200]{1,2,0:T(8,128)(2,1)S(1)}, u32[]{:S(2)}, u32[]{:S(2)}) async-start(bf16[16,128,200]{1,2,0:T(8,128)(2,1)} %fusion.18), calls=%async_computation | async-start | bytes 1638400 | tf_op jit(solution)/shard_map/all_to_all | solution.py:100
  309.3 11.9 %all-to-all-done = bf16[16,128,200]{1,2,0:T(8,128)(2,1)S(1)} async-done(((bf16[16,128,200]{1,2,0:T(8,128)(2,1)}), bf16[16,128,200]{1,2,0:T(8,128)(2,1)S(1)}, u32[]{:S(2)}, u32[]{:S(2)}) %all-to-all-start) | async-done | bytes 819232 | tf_op jit(solution)/shard_map/all_to_all | solution.py:100
  321.3 25.5 %all-gather.10.cloned.1.call-done = bf16[34816,128]{1,0:T(8,128)(2,1)} async-done(((bf16[2176,128]{1,0:T(8,128)(2,1)}), bf16[34816,128]{1,0:T(8,128)(2,1)}) %all-gather.10.cloned.1.call-update) | async-done | bytes 8912912 | tf_op jit(solution)/shard_map/all_gather | solution.py:103
  346.8 10.8 %convolution_convert_fusion.1 = bf16[16,2176,200]{1,2,0:T(8,128)(2,1)} fusion(bf16[16,2176,128]{2,1,0:T(8,128)(2,1)} %bitcast.114, bf16[16,128,200]{1,2,0:T(8,128)(2,1)S(1)} %all-to-all-done), kind=kOutput, calls=%fused_computation.8 | convolution fusion | flops 1789542400 | bytes 23658496 | tf_op jit(solution)/shard_map/hsc,hcd->hsd/dot_general | solution.py:104
  357.6 7.3 %convert_reduce_fusion = f32[2176,200]{0,1:T(8,128)S(1)} fusion(bf16[16,2176,200]{1,2,0:T(8,128)(2,1)} %convolution_convert_fusion.1), kind=kLoop, calls=%fused_computation.7 | loop fusion | flops 13491200 | bytes 15667200 | tf_op jit(solution)/shard_map/reduce_sum | solution.py:110
  368.1 4.9 copy.33
  373.0 3.9 stack_reshape.7
  376.9 4.9 copy.31
  381.7 3.8 stack_reshape.6
  386.8 3.3 broadcast_select_fusion
  390.1 5.0 all-to-all-start.1
  395.4 90.6 %all-to-all-done.1 = bf16[8,2,256,800]{2,3,1,0:T(8,128)(2,1)} async-done(((bf16[8,2,256,800]{2,3,1,0:T(8,128)(2,1)}), bf16[8,2,256,800]{2,3,1,0:T(8,128)(2,1)}, u32[]{:S(2)}, u32[]{:S(2)}) %all-to-all-start.1) | async-done | bytes 6553632 | tf_op jit(solution)/shard_map/all_to_all | solution.py:121
  486.1 11.1 %copy.34 = bf16[8,2,256,800]{3,2,1,0:T(8,128)(2,1)} copy(bf16[8,2,256,800]{2,3,1,0:T(8,128)(2,1)} %all-to-all-done.1) | data formatting | bytes 13107200 | tf_op jit(solution)/shard_map/all_to_all | solution.py:121
  497.1 14.7 %reshape.242 = bf16[16,204800]{1,0:T(8,128)(2,1)} reshape(bf16[8,2,256,800]{3,2,1,0:T(8,128)(2,1)} %copy.34) | data formatting | bytes 13107200 | tf_op jit(solution)/shard_map/reshape | solution.py:39
  511.9 4.0 convolution_convert_fusion
  517.5 2.8 reshape.243
  (68 shorter events, 28.5 us)
Async XLA Ops:
  6.5 103.6 %all-gather.8.cloned.1.call-start = ((), (), s32[]{:S(2)}) async-start(), calls=%async_computation.3 | async-start | bytes 14796800 | tf_op jit(solution)/shard_map/all_gather | solution.py:46
  7.3 158.4 %all-gather.6.cloned.1.call-start = ((), (), s32[]{:S(2)}) async-start(), calls=%async_computation.2 | async-start | bytes 2764800 | tf_op jit(solution)/shard_map/all_gather | solution.py:56
  8.0 338.8 %all-gather.10.cloned.1.call-start = ((), (), s32[]{:S(2)}) async-start(), calls=%async_computation.4 | async-start | bytes 9469952 | tf_op jit(solution)/shard_map/all_gather | solution.py:103
  8.8 156.8 %copy-start.4 = (f32[3200]{0:T(1024)S(1)}, f32[3200]{0:T(1024)}, u32[]{:S(2)}) copy-start(f32[3200]{0:T(1024)} %param.9) | copy-start | bytes 38404
  245.3 3.4 copy-start
  248.7 5.9 %copy-start.1 = (bf16[128,400]{0,1:T(8,128)(2,1)S(1)}, bf16[128,400]{0,1:T(8,128)(2,1)}, u32[]{:S(2)}) copy-start(bf16[128,400]{0,1:T(8,128)(2,1)} %param.12) | copy-start | bytes 307204
  253.6 52.0 %copy-start.2 = (s32[8,2]{0,1:T(2,128)S(1)}, s32[8,2]{0,1:T(2,128)}, u32[]{:S(2)}) copy-start(s32[8,2]{0,1:T(2,128)} %param.15) | copy-start | bytes 196
  253.6 52.0 %copy-start.3 = (s32[8,2]{0,1:T(2,128)S(1)}, s32[8,2]{0,1:T(2,128)}, u32[]{:S(2)}) copy-start(s32[8,2]{0,1:T(2,128)} %param.14) | copy-start | bytes 196
  290.0 31.3 %all-to-all-start = ((bf16[16,128,200]{1,2,0:T(8,128)(2,1)}), bf16[16,128,200]{1,2,0:T(8,128)(2,1)S(1)}, u32[]{:S(2)}, u32[]{:S(2)}) async-start(bf16[16,128,200]{1,2,0:T(8,128)(2,1)} %fusion.18), calls=%async_computation | async-start | bytes 1638400 | tf_op jit(solution)/shard_map/all_to_all | solution.py:100
  390.1 95.9 %all-to-all-start.1 = ((bf16[8,2,256,800]{2,3,1,0:T(8,128)(2,1)}), bf16[8,2,256,800]{2,3,1,0:T(8,128)(2,1)}, u32[]{:S(2)}, u32[]{:S(2)}) async-start(bf16[8,2,256,800]{2,3,1,0:T(8,128)(2,1)} %broadcast_select_fusion), calls=%async_computation.1 | async-start | bytes 13107200 | tf_op jit(solution)/shard_map/all_to_all | solution.py:121
Sparse Core Ops, SparseCore 0:
  9.8 100.3 all-gather.7
  111.8 53.8 all-gather.5
  254.7 92.0 all-gather.9
